TPU v7x, 128 devices: a whole 4x4x4 slice. The times are simulated.
128 devices in a mesh: pix: 8 (over y_hi, z), tm: 16 (over x, y_lo, core).
Axes of the slice: x: 4, y: 4 (y_hi: 2, y_lo: 2; y = y_hi * 2 + y_lo), z: 4, core: 2. Of those that a mesh axis runs over, the one named last changes fastest.
Arguments:
- frames: float32 [16, 192, 12288], P('tm', 'pix'), may hold values from 0.05 to 5
- pixel_order: int32 [12288], replicated, may hold values from 0 to 12287, each once
- cycle_sizes: int32 [64], replicated, may hold values from 1 to 384, 12288 in all
- kernel: float32 [5], replicated, may hold values from 0.1 to 1
Outputs:
- correlation: float32 [64, 3072, 3072], P('pix', 'tm')
Inputs may be any that keep to these rules, and one draw needn't show every extreme that they name: `cycle_sizes`: every cycle has one or more pixels, the sizes sum to 12288, and one cycle has exactly 384.
All inputs are finite; a program needn't handle non-finite values.
Results may differ from a plain program's by a relative error of at most 0.00005.
Values sent between devices are 32-bit elements; how exact they have to be, the bound alone decides.
No kernel may reach another device: no remote copies, remote signals or barrier semaphores. Data moves between devices by JAX's collectives and lax.ppermute only.
A program may use at most 256 MiB of HBM per device.

v0:
```python
import jax
import jax.numpy as jnp
from jax import lax
from jax.sharding import PartitionSpec as P

REACH = 2


def halo_frames(block, width):
    count = lax.axis_size("tm")
    forward = [(i, i + 1) for i in range(count - 1)]
    backward = [(i + 1, i) for i in range(count - 1)]
    n = block.shape[-1]
    low = lax.ppermute(block[..., n - width :], "tm", forward)
    high = lax.ppermute(block[..., :width], "tm", backward)
    return jnp.concatenate([low, block, high], axis=-1)


def correlate(left, right):
    return jnp.einsum(
        "rfs,rgs->rfg",
        left,
        right,
        precision=lax.Precision.HIGH,
        preferred_element_type=jnp.float32,
    )


def per_device(frames, pixel_order, cycle_sizes, kernel):
    block = frames[0]
    sub, pixels = block.shape
    cycles = cycle_sizes.shape[0]
    cap = 2 * pixels // cycles
    groups = lax.axis_size("pix")
    owned = cycles // groups
    counts = [owned - owned * 5 // 8, owned * 5 // 8]
    firsts = [sum(counts[:i]) for i in range(len(counts))]
    tblk = groups * sub
    starts = (jnp.cumsum(cycle_sizes) - cycle_sizes).astype(jnp.int32).reshape(groups, owned)
    me = lax.axis_index("pix")
    mine = lax.dynamic_index_in_dim(starts, me, 0, keepdims=False)
    sizes = lax.dynamic_index_in_dim(cycle_sizes.reshape(groups, owned), me, 0, keepdims=False)
    slots = jnp.arange(cap, dtype=jnp.int32)
    lanes = 32
    longest = max(counts) * cap + lanes
    count = pixels // lanes + longest // lanes
    order = (
        jnp.pad(pixel_order, (0, count * lanes - pixels)).reshape(count, lanes).astype(jnp.float32)
    )
    series = block.T
    outs = []
    for part, (step, first) in enumerate(zip(counts, firsts)):
        span = step * cap + lanes
        aligned = starts[:, first] // lanes * lanes
        rows = (aligned // lanes)[:, None] + jnp.arange(span // lanes, dtype=jnp.int32)
        pick_rows = (rows[..., None] == jnp.arange(count, dtype=jnp.int32)).astype(jnp.float32)
        window = jnp.einsum(
            "drk,kl->drl",
            pick_rows,
            order,
            precision=lax.Precision.HIGHEST,
            preferred_element_type=jnp.float32,
        )
        window = window.astype(jnp.int32).reshape(groups * span)
        chunks = series.at[window].get(mode="promise_in_bounds").reshape(groups, span, sub)
        got = lax.all_to_all(chunks, "pix", 0, 0, tiled=True)
        got = jnp.pad(got, ((0, 0), (0, cap), (0, 0)))
        offsets = mine[first : first + step] - mine[first] // lanes * lanes
        masks = slots[None, :] < sizes[first : first + step, None]
        picked = []
        for l in range(step):
            taken = lax.dynamic_slice_in_dim(got, offsets[l], cap, 1)
            picked.append(jnp.where(masks[l][None, :, None], taken, 0.0))
        picked = jnp.stack(picked)
        picked = jnp.transpose(picked, (0, 2, 1, 3)).reshape(step, cap, tblk)
        total = jnp.sum(picked, axis=1, keepdims=True)
        scaled = picked / total
        scale = sizes[first : first + step].astype(jnp.float32)[:, None, None]
        if part == 0:
            whole = lax.all_gather(jnp.swapaxes(scaled, 1, 2), "tm", axis=1, tiled=True)
            frames_all = whole.shape[1]
            rimmed = jnp.pad(whole, ((0, 0), (REACH, REACH), (0, 0)))
            right = kernel[0] * rimmed[:, 0:frames_all]
            for shift_step in range(1, 2 * REACH + 1):
                right = right + kernel[shift_step] * rimmed[:, shift_step : shift_step + frames_all]
            smooth = lax.dynamic_slice_in_dim(right, lax.axis_index("tm") * tblk, tblk, 1)
        else:
            rimmed = halo_frames(scaled, REACH)
            smooth = kernel[0] * rimmed[..., 0:tblk]
            for shift_step in range(1, 2 * REACH + 1):
                smooth = smooth + kernel[shift_step] * rimmed[..., shift_step : shift_step + tblk]
            smooth = jnp.swapaxes(smooth, 1, 2)
            right = lax.all_gather(smooth, "tm", axis=1, tiled=True)
        outs.append(correlate(smooth * scale, right))
    last = counts[-1]
    result = lax.optimization_barrier(
        jnp.pad(jnp.concatenate(outs[:-1], 0), ((0, last), (0, 0), (0, 0)))
    )
    return lax.dynamic_update_slice_in_dim(result, outs[-1], owned - last, 0)


def solution(mesh):
    placed = (P("tm", "pix", None), P(), P(), P())
    return jax.shard_map(
        per_device, mesh=mesh, in_specs=placed, out_specs=P("pix", "tm", None), check_vma=False
    )
```

profile of v0, /device:TPU:1, one launch (start us, length us, event | category | flops | bytes accessed | tf_op | source)
XLA Modules:
  0.0 314.3 jit_solution(2399621395003718831)
XLA Ops:
  6.5 0.8 copy.10
  7.6 0.7 sub.37
  8.3 0.2 fusion.52
  8.6 0.8 pad_convert_fusion
  9.5 0.8 convolution_convert_fusion.1
  10.8 4.0 %copy.9 = f32[1,24,12288]{1,2,0:T(8,128)} copy(f32[1,24,12288]{2,1,0:T(8,128)S(1)} %copy-done.1) | data formatting | bytes 2359296 | tf_op args[0]
  14.8 21.1 %gather_fusion = f32[9472,24]{1,0:T(8,128)} fusion(f32[12288,24]{1,0:T(8,128)} %bitcast.76, s32[10240]{0:T(1024)S(1)} %pad_clamp_fusion.1), kind=kCustom, calls=%fused_computation | custom fusion | bytes 1856512 | tf_op jit(solution)/shard_map/gather | solution.py:65
  35.8 3.9 %copy.13 = f32[8,1184,24]{1,2,0:T(8,128)} copy(f32[8,1184,24]{2,1,0:T(8,128)} %bitcast.79) | data formatting | bytes 1818624 | tf_op jit(solution)/shard_map/reshape | solution.py:65
  39.8 8.6 %all-to-all-start = ((f32[8,1184,24]{1,2,0:T(8,128)}), f32[8,1184,24]{1,2,0:T(8,128)S(1)}, u32[]{:S(2)}, u32[]{:S(2)}) async-start(f32[8,1184,24]{1,2,0:T(8,128)} %copy.13), calls=%async_computation | async-start | bytes 1966080 | tf_op jit(solution)/shard_map/all_to_all | solution.py:66
  48.5 0.6 fusion.62
  51.7 0.7 fusion.64
  58.3 3.6 %all-to-all-done = f32[8,1184,24]{1,2,0:T(8,128)S(1)} async-done(((f32[8,1184,24]{1,2,0:T(8,128)}), f32[8,1184,24]{1,2,0:T(8,128)S(1)}, u32[]{:S(2)}, u32[]{:S(2)}) %all-to-all-start) | async-done | bytes 909344 | tf_op jit(solution)/shard_map/all_to_all | solution.py:66
  61.9 0.3 fusion.21
  62.5 1.1 bitcast_divide_fusion.1
  63.7 0.9 convolution_convert_fusion
  65.2 32.3 %gather_fusion.1 = f32[15616,24]{1,0:T(8,128)} fusion(f32[12288,24]{1,0:T(8,128)} %bitcast.77, s32[16384]{0:T(1024)S(1)} %pad_clamp_fusion), kind=kCustom, calls=%fused_computation.1 | custom fusion | bytes 3060736 | tf_op jit(solution)/shard_map/gather | solution.py:65
  97.5 6.1 %copy.16 = f32[8,1952,24]{1,2,0:T(8,128)} copy(f32[8,1952,24]{2,1,0:T(8,128)} %bitcast.78) | data formatting | bytes 2998272 | tf_op jit(solution)/shard_map/reshape | solution.py:65
  103.6 5.9 %all-to-all-start.1 = ((f32[8,1952,24]{1,2,0:T(8,128)}), f32[8,1952,24]{1,2,0:T(8,128)S(1)}, u32[]{:S(2)}, u32[]{:S(2)}) async-start(f32[8,1952,24]{1,2,0:T(8,128)} %copy.16), calls=%async_computation.1 | async-start | bytes 3145728 | tf_op jit(solution)/shard_map/all_to_all | solution.py:66
  112.1 0.6 fusion.61
  122.0 25.3 %all-to-all-done.1 = f32[8,1952,24]{1,2,0:T(8,128)S(1)} async-done(((f32[8,1952,24]{1,2,0:T(8,128)}), f32[8,1952,24]{1,2,0:T(8,128)S(1)}, u32[]{:S(2)}, u32[]{:S(2)}) %all-to-all-start.1) | async-done | bytes 1499168 | tf_op jit(solution)/shard_map/all_to_all | solution.py:66
  148.1 0.2 bitcast_reduce_fusion
  148.4 0.2 bitcast_divide_fusion
  148.7 3.8 %collective-permute-start = (f32[5,384,2]{1,2,0:T(2,128)S(1)}, f32[5,384,2]{1,2,0:T(2,128)S(1)}, u32[]{:S(2)}, u32[]{:S(2)}) collective-permute-start(f32[5,384,2]{1,2,0:T(2,128)S(1)} %get-tuple-element.15), channel_id=1, source_target_pairs={{0,1},{1,2},{2,3},{3,4},{4,5},{5,6},{6,7},{7,8},{8,9},{9,10},{10,1... | collective-permute-start | bytes 46088 | tf_op jit(solution)/shard_map/ppermute | solution.py:14
  152.5 2.1 collective-permute-start.1
  154.6 0.7 fusion.63
  155.3 3.1 collective-permute-done.1
  158.4 5.0 %fusion.5 = f32[5,192,384]{2,1,0:T(8,128)} fusion(f32[5,384,192]{1,2,0:T(8,128)S(1)} %bitcast_divide_fusion, f32[5,384,2]{1,2,0:T(2,128)S(1)} %collective-permute-done.1, f32[5,384,2]{1,2,0:T(2,128)S(1)} %collective-permute-done, f32[]{:T(128)} %bitcast.20, f32[]{:T(128)} %bitcast.19, f32[]{:T(128)} %bitcast.18, f32[]{:T(128)} %bitcast.17, f32[]{:T(128)} %bitcast), kind=kLoop, calls=%fused_computation.19 | loop fusion | flops 4792320 | bytes 2979860 | tf_op jit(solution)/shard_map/transpose | solution.py:92
  163.5 33.8 %multiply_add_fusion = f32[3,3072,384]{2,1,0:T(8,128)} fusion(f32[3,3072,384]{2,1,0:T(8,128)} %all-gather.3.cloned.1.call-done, f32[]{:T(128)} %bitcast.20, f32[]{:T(128)} %bitcast.19, f32[]{:T(128)} %bitcast.18, f32[]{:T(128)} %bitcast.17, f32[]{:T(128)} %bitcast), kind=kLoop, calls=%fused_computation.2 | loop fusion | flops 31850496 | bytes 28311572 | tf_op jit(solution)/shard_map/add | solution.py:85
  197.3 13.4 %fusion.13 = f32[3,192,3072]{2,1,0:T(8,128)} fusion(f32[3,3072,384]{2,1,0:T(8,128)} %multiply_add_fusion, s32[]{:T(128)S(6)} %select_n.119, f32[3]{0:T(128)S(1)} %get-tuple-element.29), kind=kOutput, calls=%fused_computation.40 | convolution fusion | flops 4077084672 | bytes 22118416 | tf_op jit(solution)/shard_map/rfs,rgs->rfg/dot_general | solution.py:20
  210.7 12.7 %pad.23 = f32[8,192,3072]{2,1,0:T(8,128)} pad(f32[3,192,3072]{2,1,0:T(8,128)} %fusion.13, f32[]{:T(128)} %constant.86.clone.1), padding=0_5x0_0x0_0 | pad | bytes 25952260 | tf_op jit(solution)/shard_map/jit(_pad)/pad | solution.py:97
  223.5 63.8 %all-gather.5.cloned.1.call-done = f32[5,3072,384]{2,1,0:T(8,128)} async-done(((f32[5,192,384]{2,1,0:T(8,128)}), f32[5,3072,384]{2,1,0:T(8,128)}) %all-gather.5.cloned.1.call-update) | async-done | bytes 23592976 | tf_op jit(solution)/shard_map/all_gather | solution.py:93
  287.2 20.2 %convolution_dynamic-update-slice_fusion = f32[8,192,3072]{2,1,0:T(8,128)} fusion(f32[8,192,3072]{2,1,0:T(8,128)} %pad.23, f32[5,3072,384]{2,1,0:T(8,128)} %all-gather.5.cloned.1.call-done, f32[5,192,384]{2,1,0:T(8,128)S(1)} %copy-done, f32[5]{0:T(128)S(1)} %get-tuple-element.20), kind=kOutput, calls=%fused_computation.5 | convolution fusion | flops 6795141120 | bytes 36864020 | tf_op jit(solution)/shard_map/rfs,rgs->rfg/dot_general | solution.py:20
  (48 shorter events, 3.2 us)
Async XLA Ops:
  6.5 4.2 %copy-start.1 = (f32[1,24,12288]{2,1,0:T(8,128)S(1)}, f32[1,24,12288]{2,1,0:T(8,128)}, u32[]{:S(2)}) copy-start(f32[1,24,12288]{2,1,0:T(8,128)} %param.4) | copy-start | bytes 3538948
  39.8 8.7 %copy-start.3 = (s32[64]{0:T(128)S(1)}, s32[64]{0:T(128)}, u32[]{:S(2)}) copy-start(s32[64]{0:T(128)} %param.6) | copy-start | bytes 772
  39.8 22.1 %all-to-all-start = ((f32[8,1184,24]{1,2,0:T(8,128)}), f32[8,1184,24]{1,2,0:T(8,128)S(1)}, u32[]{:S(2)}, u32[]{:S(2)}) async-start(f32[8,1184,24]{1,2,0:T(8,128)} %copy.13), calls=%async_computation | async-start | bytes 1966080 | tf_op jit(solution)/shard_map/all_to_all | solution.py:66
  48.4 115.1 %all-gather.3.cloned.1.call-start = ((), (), s32[]{:S(2)}) async-start(), calls=%async_computation.2 | async-start | bytes 15040512 | tf_op jit(solution)/shard_map/all_gather | solution.py:80
  103.6 43.8 %all-to-all-start.1 = ((f32[8,1952,24]{1,2,0:T(8,128)}), f32[8,1952,24]{1,2,0:T(8,128)S(1)}, u32[]{:S(2)}, u32[]{:S(2)}) async-start(f32[8,1952,24]{1,2,0:T(8,128)} %copy.16), calls=%async_computation.1 | async-start | bytes 3145728 | tf_op jit(solution)/shard_map/all_to_all | solution.py:66
  109.5 177.7 %all-gather.5.cloned.1.call-start = ((), (), s32[]{:S(2)}) async-start(), calls=%async_computation.3 | async-start | bytes 25067520 | tf_op jit(solution)/shard_map/all_gather | solution.py:93
  148.4 6.2 %copy-start.2 = (f32[5]{0:T(128)S(1)}, f32[5]{0:T(128)}, u32[]{:S(2)}) copy-start(f32[5]{0:T(128)} %param.7) | copy-start | bytes 64
  148.7 6.6 %collective-permute-start = (f32[5,384,2]{1,2,0:T(2,128)S(1)}, f32[5,384,2]{1,2,0:T(2,128)S(1)}, u32[]{:S(2)}, u32[]{:S(2)}) collective-permute-start(f32[5,384,2]{1,2,0:T(2,128)S(1)} %get-tuple-element.15), channel_id=1, source_target_pairs={{0,1},{1,2},{2,3},{3,4},{4,5},{5,6},{6,7},{7,8},{8,9},{9,10},{10,1... | collective-permute-start | bytes 46088 | tf_op jit(solution)/shard_map/ppermute | solution.py:14
  152.5 5.9 %collective-permute-start.1 = (f32[5,384,2]{1,2,0:T(2,128)S(1)}, f32[5,384,2]{1,2,0:T(2,128)S(1)}, u32[]{:S(2)}, u32[]{:S(2)}) collective-permute-start(f32[5,384,2]{1,2,0:T(2,128)S(1)} %get-tuple-element.16), channel_id=1, source_target_pairs={{1,0},{2,1},{3,2},{4,3},{5,4},{6,5},{7,6},{8,7},{9,8},{10,9},{11,1... | collective-permute-start | bytes 46088 | tf_op jit(solution)/shard_map/ppermute | solution.py:15
  210.7 76.5 %copy-start = (f32[5,192,384]{2,1,0:T(8,128)S(1)}, f32[5,192,384]{2,1,0:T(8,128)}, u32[]{:S(2)}) copy-start(f32[5,192,384]{2,1,0:T(8,128)} %fusion.5) | copy-start | bytes 4423684
Sparse Core Ops, SparseCore 0:
  63.7 97.0 all-gather.2
  163.6 123.6 all-gather.4
where the time goes:
time: 315 us; the launch traced here: 314 us
  waiting for transfers between devices  95.8 us (30%)
  local copies, waits for them, and re-layouts  84.6 us (27%)
  other arithmetic  44.3 us (14%)
  matrix products  35.4 us (11%)
  between operations  33.7 us (11%)
  starting transfers between devices  20.5 us (7%)
    all_gather x1, waiting for transfers between devices, per_device(): right = lax.all_gather(smooth, 'tm', axis=1, tiled=True)  63.8 us
    gather x2, local copies, waits for them, and re-layouts, per_device(): series.at[window].get(mode='promise_in_bounds').reshape(groups, span, sub)  53.4 us
    add x1, other arithmetic, per_device(): right + kernel[shift_step] * rimmed[:, shift_step:shift_step + frames_all]  33.8 us
    dot_general x2, matrix products, correlate(): jnp.einsum('rfs,rgs->rfg', left, right, precision=lax.Precision.HIGH, pre...  33.6 us
    all_to_all x2, waiting for transfers between devices, per_device(): got = lax.all_to_all(chunks, 'pix', 0, 0, tiled=True)  28.9 us
    all_to_all x2, starting transfers between devices, per_device(): got = lax.all_to_all(chunks, 'pix', 0, 0, tiled=True)  14.5 us
    pad x1, local copies, waits for them, and re-layouts, per_device(): jnp.pad(jnp.concatenate(outs[:-1], 0), ((0, last), (0, 0), (0, 0)))  12.7 us
    reshape x2, local copies, waits for them, and re-layouts, per_device(): series.at[window].get(mode='promise_in_bounds').reshape(groups, span, sub)  10 us
  transfers between devices with their start and end apart: 6, of which 4 were waited for; matrix products, arithmetic and copies ran while one was open for 35% of the time, Pallas kernels for 0%

commit v1 on v0

--- a/solution.py
+++ b/solution.py
@@ -90,7 +90,9 @@
             for shift_step in range(1, 2 * REACH + 1):
                 smooth = smooth + kernel[shift_step] * rimmed[..., shift_step : shift_step + tblk]
             smooth = jnp.swapaxes(smooth, 1, 2)
-            right = lax.all_gather(smooth, "tm", axis=1, tiled=True)
+            right = jnp.concatenate(
+                lax.all_to_all(jnp.stack([smooth] * lax.axis_size("tm")), "tm", 0, 0), axis=1
+            )
         outs.append(correlate(smooth * scale, right))
     last = counts[-1]
     result = lax.optimization_barrier(

time: 315 us -> 667 us (2.12)
  waiting for transfers between devices: 95.8 us -> 416 us
  local copies, waits for them, and re-layouts: 84.6 us -> 113 us
    all_to_all x0 -> x1, waiting for transfers between devices: none -> 384 us  [per_device(): lax.all_to_all(jnp.stack([smooth] * lax.axis_size('tm')), 'tm', 0, 0)]
    all_gather x1 -> x0, waiting for transfers between devices: 63.8 us -> none  [per_device(): right = lax.all_gather(smooth, 'tm', axis=1, tiled=True)]
    reshape x0 -> x1, local copies, waits for them, and re-layouts: none -> 16.7 us  [per_device(): jnp.concatenate(lax.all_to_all(jnp.stack([smooth] * lax.axis_size('tm')),...]
    another operation x1 -> x2, local copies, waits for them, and re-layouts: 0.84 us -> 11.4 us  [the longest x1 10.7 us: per_device(): jnp.stack([smooth] * lax.axis_size('tm'))]
  transfers between devices with their start and end apart: 6 -> 6, of which waited for: 4 -> 4; matrix products, arithmetic and copies ran while one was open for 35% -> 11% of each run, Pallas kernels for 0% -> 0%
where the time goes in v1:
time: 667 us; the launch traced here: 666 us
  waiting for transfers between devices  416 us (62%)
  local copies, waits for them, and re-layouts  113 us (17%)
  other arithmetic  41.6 us (6%)
  matrix products  35.2 us (5%)
  between operations  34 us (5%)
  starting transfers between devices  26.1 us (4%)
    all_to_all x1, waiting for transfers between devices, per_device(): lax.all_to_all(jnp.stack([smooth] * lax.axis_size('tm')), 'tm', 0, 0)  384 us
    gather x2, local copies, waits for them, and re-layouts, per_device(): series.at[window].get(mode='promise_in_bounds').reshape(groups, span, sub)  53.4 us
    dot_general x2, matrix products, correlate(): jnp.einsum('rfs,rgs->rfg', left, right, precision=lax.Precision.HIGH, pre...  33.4 us
    add x1, other arithmetic, per_device(): right + kernel[shift_step] * rimmed[:, shift_step:shift_step + frames_all]  32.3 us
    all_to_all x2, waiting for transfers between devices, per_device(): got = lax.all_to_all(chunks, 'pix', 0, 0, tiled=True)  28.5 us
    reshape x1, local copies, waits for them, and re-layouts, per_device(): jnp.concatenate(lax.all_to_all(jnp.stack([smooth] * lax.axis_size('tm')),...  16.7 us
    all_to_all x2, starting transfers between devices, per_device(): got = lax.all_to_all(chunks, 'pix', 0, 0, tiled=True)  14.5 us
  transfers between devices with their start and end apart: 6, of which 4 were waited for; matrix products, arithmetic and copies ran while one was open for 11% of the time, Pallas kernels for 0%

profile of v1, /device:TPU:1, one launch (start us, length us, event | category | flops | bytes accessed | tf_op | source)
XLA Modules:
  0.0 665.7 jit_solution(715000178404263284)
XLA Ops:
  6.5 0.7 copy.18
  7.5 0.7 sub.37
  8.4 0.8 pad_convert_fusion
  9.4 4.9 copy.17
  14.3 0.8 convolution_convert_fusion.1
  15.6 21.1 %gather_fusion = f32[9472,24]{1,0:T(8,128)} fusion(f32[12288,24]{1,0:T(8,128)} %bitcast.78, s32[10240]{0:T(1024)S(1)} %pad_clamp_fusion.1), kind=kCustom, calls=%fused_computation | custom fusion | bytes 1856512 | tf_op jit(solution)/shard_map/gather | solution.py:65
  36.6 3.9 copy.21
  40.6 8.6 %all-to-all-start = ((f32[8,1184,24]{1,2,0:T(8,128)}), f32[8,1184,24]{1,2,0:T(8,128)S(1)}, u32[]{:S(2)}, u32[]{:S(2)}) async-start(f32[8,1184,24]{1,2,0:T(8,128)} %copy.21), calls=%async_computation | async-start | bytes 1966080 | tf_op jit(solution)/shard_map/all_to_all | solution.py:66
  49.3 0.7 fusion.62
  52.6 0.7 fusion.64
  59.2 3.5 all-to-all-done
  62.7 0.3 fusion.21
  63.3 1.1 bitcast_divide_fusion.1
  64.5 0.9 convolution_convert_fusion
  66.0 32.3 %gather_fusion.1 = f32[15616,24]{1,0:T(8,128)} fusion(f32[12288,24]{1,0:T(8,128)} %bitcast.79, s32[16384]{0:T(1024)S(1)} %pad_clamp_fusion), kind=kCustom, calls=%fused_computation.1 | custom fusion | bytes 3060736 | tf_op jit(solution)/shard_map/gather | solution.py:65
  98.3 6.1 copy.24
  104.4 5.9 all-to-all-start.1
  112.9 0.7 fusion.61
  123.2 24.9 %all-to-all-done.1 = f32[8,1952,24]{1,2,0:T(8,128)S(1)} async-done(((f32[8,1952,24]{1,2,0:T(8,128)}), f32[8,1952,24]{1,2,0:T(8,128)S(1)}, u32[]{:S(2)}, u32[]{:S(2)}) %all-to-all-start.1) | async-done | bytes 1499168 | tf_op jit(solution)/shard_map/all_to_all | solution.py:66
  149.5 3.8 collective-permute-start
  153.3 1.9 collective-permute-start.1
  155.2 0.7 fusion.63
  155.9 3.3 collective-permute-done.1
  159.2 3.9 fusion.5
  163.1 10.7 %stack.59 = f32[16,5,192,384]{3,2,1,0:T(8,128)} broadcast(f32[5,192,384]{2,1,0:T(8,128)S(1)} %fusion.5), dimensions={1,2,3} | broadcast | bytes 25067520 | tf_op jit(solution)/shard_map/stack | solution.py:94
  173.8 5.9 all-to-all-start.2
  179.7 384.3 %all-to-all-done.2 = f32[16,5,192,384]{3,2,1,0:T(8,128)} async-done(((f32[16,5,192,384]{3,2,1,0:T(8,128)}), f32[16,5,192,384]{3,2,1,0:T(8,128)}, u32[]{:S(2)}, u32[]{:S(2)}) %all-to-all-start.2) | async-done | bytes 23592992 | tf_op jit(solution)/shard_map/all_to_all | solution.py:94
  564.0 16.7 %copy.25 = f32[5,16,192,384]{3,2,1,0:T(8,128)} copy(f32[5,16,192,384]{3,2,0,1:T(8,128)} %bitcast.39) | data formatting | bytes 47185920 | tf_op jit(solution)/shard_map/reshape | solution.py:93
  580.7 32.3 %multiply_add_fusion = f32[3,3072,384]{2,1,0:T(8,128)} fusion(f32[3,3072,384]{2,1,0:T(8,128)} %all-gather.2.cloned.1.call-done, f32[]{:T(128)} %bitcast.20, f32[]{:T(128)} %bitcast.19, f32[]{:T(128)} %bitcast.18, f32[]{:T(128)} %bitcast.17, f32[]{:T(128)} %bitcast), kind=kLoop, calls=%fused_computation.2 | loop fusion | flops 31850496 | bytes 28311572 | tf_op jit(solution)/shard_map/add | solution.py:85
  612.9 13.2 %fusion.13 = f32[3,192,3072]{2,1,0:T(8,128)} fusion(f32[3,3072,384]{2,1,0:T(8,128)} %multiply_add_fusion, s32[]{:T(128)S(6)} %select_n.119, f32[3]{0:T(128)S(1)} %get-tuple-element.29), kind=kOutput, calls=%fused_computation.40 | convolution fusion | flops 4077084672 | bytes 22118416 | tf_op jit(solution)/shard_map/rfs,rgs->rfg/dot_general | solution.py:20
  626.2 12.5 %pad.23 = f32[8,192,3072]{2,1,0:T(8,128)} pad(f32[3,192,3072]{2,1,0:T(8,128)} %fusion.13, f32[]{:T(128)} %constant.86.clone.1), padding=0_5x0_0x0_0 | pad | bytes 25952260 | tf_op jit(solution)/shard_map/jit(_pad)/pad | solution.py:99
  638.7 20.2 %convolution_dynamic-update-slice_fusion = f32[8,192,3072]{2,1,0:T(8,128)} fusion(f32[8,192,3072]{2,1,0:T(8,128)} %pad.23, f32[5,3072,384]{2,1,0:T(8,128)} %bitcast.80, f32[5,192,384]{2,1,0:T(8,128)S(1)} %fusion.5, f32[5]{0:T(128)S(1)} %get-tuple-element.20), kind=kOutput, calls=%fused_computation.5 | convolution fusion | flops 6795141120 | bytes 36864020 | tf_op jit(solution)/shard_map/rfs,rgs->rfg/dot_general | solution.py:20
  (45 shorter events, 3.7 us)
Async XLA Ops:
  40.6 8.7 %copy-start.1 = (s32[64]{0:T(128)S(1)}, s32[64]{0:T(128)}, u32[]{:S(2)}) copy-start(s32[64]{0:T(128)} %param.6) | copy-start | bytes 772
  40.6 22.1 %all-to-all-start = ((f32[8,1184,24]{1,2,0:T(8,128)}), f32[8,1184,24]{1,2,0:T(8,128)S(1)}, u32[]{:S(2)}, u32[]{:S(2)}) async-start(f32[8,1184,24]{1,2,0:T(8,128)} %copy.21), calls=%async_computation | async-start | bytes 1966080 | tf_op jit(solution)/shard_map/all_to_all | solution.py:66
  49.2 531.5 %all-gather.2.cloned.1.call-start = ((), (), s32[]{:S(2)}) async-start(), calls=%async_computation.3 | async-start | bytes 15040512 | tf_op jit(solution)/shard_map/all_gather | solution.py:80
  104.4 43.8 %all-to-all-start.1 = ((f32[8,1952,24]{1,2,0:T(8,128)}), f32[8,1952,24]{1,2,0:T(8,128)S(1)}, u32[]{:S(2)}, u32[]{:S(2)}) async-start(f32[8,1952,24]{1,2,0:T(8,128)} %copy.24), calls=%async_computation.1 | async-start | bytes 3145728 | tf_op jit(solution)/shard_map/all_to_all | solution.py:66
  149.2 6.1 copy-start
  149.5 6.4 collective-permute-start
  153.3 5.9 collective-permute-start.1
  173.8 390.1 %all-to-all-start.2 = ((f32[16,5,192,384]{3,2,1,0:T(8,128)}), f32[16,5,192,384]{3,2,1,0:T(8,128)}, u32[]{:S(2)}, u32[]{:S(2)}) async-start(f32[16,5,192,384]{3,2,1,0:T(8,128)} %stack.59), calls=%async_computation.2 | async-start | bytes 47185920 | tf_op jit(solution)/shard_map/all_to_all | solution.py:94
Sparse Core Ops, SparseCore 0:
  64.6 97.0 all-gather.1
